TPU v7x, 32 devices: a whole 2x2x4 slice. The times are simulated.
32 devices in a mesh: island: 4 (over z), fsdp: 8 (over y, x, core).
Axes of the slice: x: 2, y: 2, z: 4, core: 2. Of those that a mesh axis runs over, the one named last changes fastest.
Arguments:
- activations: bfloat16 [4, 4096, 8192], P('island', 'fsdp'), may hold values from -150 to 150
- key_cotangents: bfloat16 [4, 4096, 512], P('island', 'fsdp'), may hold values from -60 to 60
- master: float32 [8192, 512], P('fsdp'), may hold values from -6 to 6
- momentum: float32 [8192, 512], P('fsdp'), may hold values from -3 to 3
- island_weights: float32 [4, 8192, 512], P('island', 'fsdp'), may hold values from -6 to 6
- first_moment: float32 [4, 8192, 512], P('island', 'fsdp'), may hold values from -0.0024414062 to 0.0024414062
- second_moment: float32 [4, 8192, 512], P('island', 'fsdp'), may hold values from 5.9604645e-08 to 9.536743e-07
- tile_rows: int32 [48], replicated, may hold values from 1 to 512, 8192 in all
Outputs:
- master_out: float32 [8192, 512], P('fsdp')
- momentum_out: float32 [8192, 512], P('fsdp')
- tile_sums: float32 [48], replicated
Inputs may be any that keep to these rules, and one draw needn't show every extreme that they name: `tile_rows`: consecutive tiles covering all 8192 rows; the largest has exactly 512 rows.
All inputs are finite; a program needn't handle non-finite values.
Results may differ from a plain program's by a relative error of at most 0.0003.
Values may be sent and summed in bfloat16 or wider, within the bound.
No kernel may reach another device: no remote copies, remote signals or barrier semaphores. Data moves between devices by JAX's collectives and lax.ppermute only.
A program may use at most 128 MiB of HBM per device.

v0:
```python
import jax
import jax.numpy as jnp
from jax import lax
from jax.experimental.layout import Layout, with_layout_constraint
from jax.sharding import PartitionSpec as P

HEAD = 128
SEQ = 8192
beta_one = 0.9
beta_two = 0.95
bias_one = 1.0 - 0.9**3
bias_two = 1.0 - 0.95**3
inner_rate = 0.5
decay_rate = 0.1
outer_rate = 0.7
outer_moment = 0.9
adam_eps = 1e-08
norm_epsilon = 1e-06
rope_base = 500000.0


def unrotate(cotangent, first_row):
    rows = cotangent.shape[0]
    half = HEAD // 2
    positions = ((first_row + jnp.arange(rows, dtype=jnp.int32)) % SEQ).astype(jnp.float32)
    rates = rope_base ** (-2.0 * jnp.arange(half).astype(jnp.float32) / HEAD)
    angles = positions[:, None] * rates[None, :]
    cosine = jnp.cos(angles)[:, None, :]
    sine = jnp.sin(angles)[:, None, :]
    heads = cotangent.astype(jnp.float32).reshape(rows, -1, HEAD)
    lower = heads[:, :, :half]
    upper = heads[:, :, half:]
    turned = jnp.concatenate([lower * cosine + upper * sine, upper * cosine - lower * sine], axis=2)
    return turned.reshape(rows, -1).astype(jnp.bfloat16)


def adam_update(gradient, weights, first, second):
    first_new = beta_one * first + (1.0 - beta_one) * gradient
    second_new = beta_two * second + (1.0 - beta_two) * gradient * gradient
    ratio = first_new / bias_one / (jnp.sqrt(second_new / bias_two) + adam_eps)
    return weights - inner_rate * (ratio + decay_rate * weights)


def local_tiles(drift_rows, tile_rows, first_row):
    ends = jnp.cumsum(tile_rows, dtype=jnp.int32)
    starts = ends - tile_rows
    rows = first_row + jnp.arange(drift_rows.shape[0], dtype=jnp.int32)
    member = ((rows[:, None] >= starts[None, :]) & (rows[:, None] < ends[None, :])).astype(
        jnp.float32
    )
    return jnp.dot(jnp.sum(drift_rows, axis=1), member, precision=lax.Precision.HIGHEST)


def island_sum(values, replicas, pieces=4):
    if replicas != 4:
        return lax.psum(values, "island")
    island = lax.axis_index("island")
    middle = (island == 1) | (island == 2)
    rows = values.shape[0] // pieces
    sums, arrived = ([], None)
    for piece in range(pieces):
        part = values[piece * rows : (piece + 1) * rows]
        if arrived is not None:
            part, _ = lax.optimization_barrier((part, arrived))
        arrived = lax.ppermute(part, "island", [(0, 1), (3, 2)])
        pair = part + arrived
        whole = pair + lax.ppermute(pair, "island", [(1, 2), (2, 1)])
        back = lax.ppermute(whole, "island", [(1, 0), (2, 3)])
        sums.append(jnp.where(middle, whole, back))
    return jnp.concatenate(sums, axis=0)


def body(
    activations,
    key_cotangents,
    master,
    momentum,
    island_weights,
    first_moment,
    second_moment,
    tile_rows,
):
    own_rows = master.shape[0]
    tok_rows = key_cotangents.shape[1]
    chips = lax.axis_size("chip")
    core = lax.axis_index("core")
    position = lax.axis_index("chip") * 2 + core
    swap = [(0, 1), (1, 0)]
    unrotated = unrotate(key_cotangents[0], position * tok_rows)
    tokens = activations[0]

    def parity(side):
        return jnp.stack(
            [
                lax.dynamic_slice_in_dim(tokens, (2 * k + side) * own_rows, own_rows, axis=1)
                for k in range(chips)
            ],
            axis=1,
        )

    their_tokens = lax.ppermute(parity(1 - core), "core", swap)
    their_unrotated = lax.ppermute(unrotated, "core", swap)
    contract = (((0,), (0,)), ((), ()))
    partial = lax.dot_general(
        unrotated, parity(core), contract, preferred_element_type=jnp.float32
    ) + lax.dot_general(their_unrotated, their_tokens, contract, preferred_element_type=jnp.float32)
    gradient = lax.psum_scatter(partial, "chip", scatter_dimension=1, tiled=True)
    gradient = with_layout_constraint(gradient, Layout((0, 1, 2)))
    gradient = with_layout_constraint(
        gradient.reshape(gradient.shape[0], own_rows).T, Layout((0, 1))
    )
    squares = lax.psum(jnp.sum(gradient * gradient), ("chip", "core"))
    factor = 1.0 / jnp.sqrt(squares + norm_epsilon)
    inner = adam_update(gradient * factor, island_weights[0], first_moment[0], second_moment[0])
    island_drift = master - inner
    replicas = lax.axis_size("island")
    first_row = position * own_rows
    everyone = ("island", "chip", "core")
    partials = local_tiles(island_drift, tile_rows, first_row)
    padded = jnp.zeros((65536,), jnp.float32).at[: partials.shape[0]].set(partials)
    totals = lax.psum(padded, everyone)[: partials.shape[0]] / replicas
    drift = island_sum(island_drift, replicas) / replicas
    momentum_out = outer_moment * momentum + drift
    master_out = master - outer_rate * (drift + outer_moment * momentum_out)
    tile_sums = totals / jnp.sqrt(tile_rows.astype(jnp.float32) * master.shape[1])
    return (master_out, momentum_out, tile_sums)


def solution(mesh):
    islands, fsdp = mesh.devices.shape
    cores = jax.sharding.Mesh(
        mesh.devices.reshape(islands, fsdp // 2, 2), ("island", "chip", "core")
    )
    rows = ("chip", "core")
    placed = (
        P("island", rows, None),
        P("island", rows, None),
        P(rows, None),
        P(rows, None),
        P("island", rows, None),
        P("island", rows, None),
        P("island", rows, None),
        P(),
    )
    return jax.shard_map(
        body,
        mesh=cores,
        in_specs=placed,
        out_specs=(P(rows, None), P(rows, None), P()),
        check_vma=False,
    )
```

profile of v0, /device:TPU:0, one launch (start us, length us, event | category | flops | bytes accessed | tf_op | source)
XLA Modules:
  0.0 363.9 jit_solution(9505688208822841466)
XLA Ops:
  7.2 5.7 %dynamic-slice_bitcast_fusion.3 = (bf16[512,1,1024]{2,0,1:T(8,128)(2,1)S(1)}, bf16[512,1,1024]{2,0,1:T(8,128)(2,1)S(1)}, bf16[512,1,1024]{2,0,1:T(8,128)(2,1)S(1...) fusion(bf16[1,512,8192]{2,1,0:T(8,128)(2,1)} %param.10, ...), kind=kLoop, calls=%fused_computation.32 | loop fusion | bytes 16777248 | tf_op jit(solution)/shard_map/stack | solution.py:93
  13.0 2.2 pad_maximum_fusion
  18.4 2.5 fusion
  20.9 2.2 collective-permute-done
  23.1 7.9 %convolution_add_fusion = f32[512,4,1024]{2,0,1:T(8,128)} fusion(f32[512,4,1024]{2,0,1:T(8,128)S(1)} %fusion, bf16[512,4,1024]{2,0,1:T(8,128)(2,1)} %collective-permute-done.1, bf16[512,512]{0,1:T(8,128)(2,1)S(1)} %collective-permute-done), kind=kOutput, calls=%fused_computation.10 | convolution fusion | flops 2149580800 | bytes 21495808 | tf_op jit(solution)/shard_map/dot_general | solution.py:106
  31.1 89.1 %reduce-scatter.4.cloned.1.call-done = f32[512,1,1024]{2,0,1:T(8,128)} async-done(((f32[512,4,1024]{2,0,1:T(8,128)}), f32[512,1,1024]{2,0,1:T(8,128)}) %reduce-scatter.4.cloned.1.call-update) | async-done | bytes 2097168
  120.2 1.9 copy.26
  123.3 13.3 %psum.14 = f32[]{:T(128)} all-reduce(f32[]{:T(128)} %fusion.14), channel_id=1, replica_groups=mesh['island'=4,'chip'=4,'core'=2] {'chip','core'}, use_global_device_ids=true, to_apply=%region_2.3 | all-reduce | flops 1 | bytes 8 | tf_op jit(solution)/shard_map/psum | solution.py:112
  137.2 5.4 %fusion.26 = (f32[1024]{0:T(1024)S(1)}, f32[1024,512]{1,0:T(8,128)S(1)}) fusion(f32[1024,512]{1,0:T(8,128)} %param.12, f32[1,1024,512]{2,1,0:T(8,128)} %param.16, f32[]{:T(128)S(6)} %sqrt.9, f32[512,1,1024]{0,2,1:T(8,128)S(1)} %copy.26, f32[1,1024,512]{2,1,0:T(8,128)} %param.15, f32[1,1024,512]{2,1,0:T(8,128)} %param.14), kind=kLoop, calls=%fused_computation.63 | loop fusion | flops 9436160 | bytes 12587012 | tf_op jit(solution)/shard_map/reduce_sum | solution.py:51
  142.7 3.4 collective-permute-start.2
  146.1 10.3 %collective-permute-done.2 = f32[256,512]{1,0:T(8,128)S(1)} collective-permute-done((f32[256,512]{1,0:T(8,128)S(1)}, f32[256,512]{1,0:T(8,128)S(1)}, u32[]{:S(2)}, u32[]{:S(2)}) %collective-permute-start.2) | collective-permute-done | bytes 524320 | tf_op jit(solution)/shard_map/ppermute | solution.py:65
  156.7 4.4 %collective-permute-start.5 = (f32[256,512]{1,0:T(8,128)S(1)}, f32[256,512]{1,0:T(8,128)S(1)}, u32[]{:S(2)}, u32[]{:S(2)}) collective-permute-start(f32[256,512]{1,0:T(8,128)S(1)} %get-tuple-element.18), channel_id=1, source_target_pairs={{0,8},{24,16},{1,9},{25,17},{2,10},{26,18},{3,11},{27,19},{4,12},{... | collective-permute-start | bytes 1572872 | tf_op jit(solution)/shard_map/ppermute | solution.py:65
  161.1 9.4 %collective-permute-done.5 = f32[256,512]{1,0:T(8,128)S(1)} collective-permute-done((f32[256,512]{1,0:T(8,128)S(1)}, f32[256,512]{1,0:T(8,128)S(1)}, u32[]{:S(2)}, u32[]{:S(2)}) %collective-permute-start.5) | collective-permute-done | bytes 524320 | tf_op jit(solution)/shard_map/ppermute | solution.py:65
  170.5 4.4 %collective-permute-start.8 = (f32[256,512]{1,0:T(8,128)S(1)}, f32[256,512]{1,0:T(8,128)S(1)}, u32[]{:S(2)}, u32[]{:S(2)}) collective-permute-start(f32[256,512]{1,0:T(8,128)S(1)} %get-tuple-element.19), channel_id=1, source_target_pairs={{0,8},{24,16},{1,9},{25,17},{2,10},{26,18},{3,11},{27,19},{4,12},{... | collective-permute-start | bytes 1572872 | tf_op jit(solution)/shard_map/ppermute | solution.py:65
  174.9 1.5 collective-permute-start.3
  176.4 7.0 %collective-permute-done.8 = f32[256,512]{1,0:T(8,128)S(1)} collective-permute-done((f32[256,512]{1,0:T(8,128)S(1)}, f32[256,512]{1,0:T(8,128)S(1)}, u32[]{:S(2)}, u32[]{:S(2)}) %collective-permute-start.8) | collective-permute-done | bytes 524320 | tf_op jit(solution)/shard_map/ppermute | solution.py:65
  183.4 5.4 %collective-permute-start.11 = (f32[256,512]{1,0:T(8,128)S(1)}, f32[256,512]{1,0:T(8,128)}, u32[]{:S(2)}, u32[]{:S(2)}) collective-permute-start(f32[256,512]{1,0:T(8,128)S(1)} %get-tuple-element.20), channel_id=1, source_target_pairs={{0,8},{24,16},{1,9},{25,17},{2,10},{26,18},{3,11},{27,19},{4,12},{... | collective-permute-start | bytes 1572872 | tf_op jit(solution)/shard_map/ppermute | solution.py:65
  188.8 1.4 collective-permute-start.6
  196.7 1.5 collective-permute-start.12
  200.6 126.3 %all-reduce.4.cloned.1.call-done = f32[65536]{0:T(1024)} async-done(((f32[65536]{0:T(1024)}), f32[65536]{0:T(1024)}) %all-reduce.4.cloned.1.call-update) | async-done | bytes 262160 | tf_op jit(solution)/shard_map/psum | solution.py:121
  331.8 1.6 collective-permute-start.13
  334.5 10.4 %collective-permute-done.10 = f32[256,512]{1,0:T(8,128)S(1)} collective-permute-done((f32[256,512]{1,0:T(8,128)S(1)}, f32[256,512]{1,0:T(8,128)S(1)}, u32[]{:S(2)}, u32[]{:S(2)}) %collective-permute-start.10) | collective-permute-done | bytes 524320 | tf_op jit(solution)/shard_map/ppermute | solution.py:68
  345.0 9.2 %collective-permute-done.13 = f32[256,512]{1,0:T(8,128)S(1)} collective-permute-done((f32[256,512]{1,0:T(8,128)S(1)}, f32[256,512]{1,0:T(8,128)S(1)}, u32[]{:S(2)}, u32[]{:S(2)}) %collective-permute-start.13) | collective-permute-done | bytes 524320 | tf_op jit(solution)/shard_map/ppermute | solution.py:68
  354.3 2.8 multiply_subtract_fusion
  (56 shorter events, 19.7 us)
Async XLA Ops:
  7.2 113.1 %reduce-scatter.4.cloned.1.call-start = ((), (), s32[]{:S(2)}) async-start(), calls=%async_computation.2 | async-start | bytes 10485760
  15.2 8.0 %collective-permute-start.1 = (bf16[512,4,1024]{2,0,1:T(8,128)(2,1)}, bf16[512,4,1024]{2,0,1:T(8,128)(2,1)}, u32[]{:S(2)}, u32[]{:S(2)}) collective-permute-start(bf16[512,4,1024]{2,0,1:T(8,128)(2,1)} %pad_maximum_fusion), channel_id=1, source_target_pairs={{0,1},{1,0},{2,3},{3,2},{4,5},{5,4},{6,7},{7,6},{8,9},{9,8},{10,11... | collective-permute-start | bytes 12582920 | tf_op jit(solution)/shard_map/ppermute | solution.py:101
  16.9 1.2 copy-start.2
  16.9 1.5 copy-start.3
  17.7 5.5 %collective-permute-start = (bf16[512,512]{0,1:T(8,128)(2,1)S(1)}, bf16[512,512]{0,1:T(8,128)(2,1)S(1)}, u32[]{:S(2)}, u32[]{:S(2)}) collective-permute-start(bf16[512,512]{0,1:T(8,128)(2,1)S(1)} %bitcast.66), channel_id=1, source_target_pairs={{0,1},{1,0},{2,3},{3,2},{4,5},{5,4},{6,7},{7,6},{8,9},{9,8},{10,11... | collective-permute-start | bytes 1572872 | tf_op jit(solution)/shard_map/ppermute | solution.py:102
  31.0 295.9 %all-reduce.4.cloned.1.call-start = ((), (), s32[]{:S(2)}) async-start(), calls=%async_computation.1 | async-start | bytes 524288 | tf_op jit(solution)/shard_map/psum | solution.py:121
  142.7 13.7 %collective-permute-start.2 = (f32[256,512]{1,0:T(8,128)S(1)}, f32[256,512]{1,0:T(8,128)S(1)}, u32[]{:S(2)}, u32[]{:S(2)}) collective-permute-start(f32[256,512]{1,0:T(8,128)S(1)} %slice.41), channel_id=1, source_target_pairs={{0,8},{24,16},{1,9},{25,17},{2,10},{26,18},{3,11},{27,19},{4,12},{... | collective-permute-start | bytes 1572872 | tf_op jit(solution)/shard_map/ppermute | solution.py:65
  156.7 13.8 %collective-permute-start.5 = (f32[256,512]{1,0:T(8,128)S(1)}, f32[256,512]{1,0:T(8,128)S(1)}, u32[]{:S(2)}, u32[]{:S(2)}) collective-permute-start(f32[256,512]{1,0:T(8,128)S(1)} %get-tuple-element.18), channel_id=1, source_target_pairs={{0,8},{24,16},{1,9},{25,17},{2,10},{26,18},{3,11},{27,19},{4,12},{... | collective-permute-start | bytes 1572872 | tf_op jit(solution)/shard_map/ppermute | solution.py:65
  170.5 12.9 %collective-permute-start.8 = (f32[256,512]{1,0:T(8,128)S(1)}, f32[256,512]{1,0:T(8,128)S(1)}, u32[]{:S(2)}, u32[]{:S(2)}) collective-permute-start(f32[256,512]{1,0:T(8,128)S(1)} %get-tuple-element.19), channel_id=1, source_target_pairs={{0,8},{24,16},{1,9},{25,17},{2,10},{26,18},{3,11},{27,19},{4,12},{... | collective-permute-start | bytes 1572872 | tf_op jit(solution)/shard_map/ppermute | solution.py:65
  174.9 15.3 %collective-permute-start.3 = (f32[256,512]{1,0:T(8,128)S(1)}, f32[256,512]{1,0:T(8,128)}, u32[]{:S(2)}, u32[]{:S(2)}) collective-permute-start(f32[256,512]{1,0:T(8,128)S(1)} %get-tuple-element.33), channel_id=1, source_target_pairs={{8,16},{16,8},{9,17},{17,9},{10,18},{18,10},{11,19},{19,11},{12,20... | collective-permute-start | bytes 1572872 | tf_op jit(solution)/shard_map/ppermute | solution.py:67
  183.4 10.1 %copy-start.4 = (s32[48]{0:T(128)S(1)}, s32[48]{0:T(128)}, u32[]{:S(2)}) copy-start(s32[48]{0:T(128)} %param.17) | copy-start | bytes 580
  183.4 12.2 %collective-permute-start.11 = (f32[256,512]{1,0:T(8,128)S(1)}, f32[256,512]{1,0:T(8,128)}, u32[]{:S(2)}, u32[]{:S(2)}) collective-permute-start(f32[256,512]{1,0:T(8,128)S(1)} %get-tuple-element.20), channel_id=1, source_target_pairs={{0,8},{24,16},{1,9},{25,17},{2,10},{26,18},{3,11},{27,19},{4,12},{... | collective-permute-start | bytes 1572872 | tf_op jit(solution)/shard_map/ppermute | solution.py:65
  188.8 9.4 %collective-permute-start.6 = (f32[256,512]{1,0:T(8,128)S(1)}, f32[256,512]{1,0:T(8,128)}, u32[]{:S(2)}, u32[]{:S(2)}) collective-permute-start(f32[256,512]{1,0:T(8,128)S(1)} %add.170), channel_id=1, source_target_pairs={{8,16},{16,8},{9,17},{17,9},{10,18},{18,10},{11,19},{19,11},{12,20... | collective-permute-start | bytes 1572872 | tf_op jit(solution)/shard_map/ppermute | solution.py:67
  191.4 138.1 %collective-permute-start.4 = (f32[256,512]{1,0:T(8,128)S(1)}, f32[256,512]{1,0:T(8,128)}, u32[]{:S(2)}, u32[]{:S(2)}) collective-permute-start(f32[256,512]{1,0:T(8,128)S(1)} %add.169), channel_id=1, source_target_pairs={{8,0},{16,24},{9,1},{17,25},{10,2},{18,26},{11,3},{19,27},{12,4},{... | collective-permute-start | bytes 1572872 | tf_op jit(solution)/shard_map/ppermute | solution.py:68
  192.8 135.3 %collective-permute-start.9 = (f32[256,512]{1,0:T(8,128)S(1)}, f32[256,512]{1,0:T(8,128)S(1)}, u32[]{:S(2)}, u32[]{:S(2)}) collective-permute-start(f32[256,512]{1,0:T(8,128)S(1)} %add.172), channel_id=1, source_target_pairs={{8,16},{16,8},{9,17},{17,9},{10,18},{18,10},{11,19},{19,11},{12,20... | collective-permute-start | bytes 1572872 | tf_op jit(solution)/shard_map/ppermute | solution.py:67
  196.7 134.0 %collective-permute-start.12 = (f32[256,512]{1,0:T(8,128)S(1)}, f32[256,512]{1,0:T(8,128)}, u32[]{:S(2)}, u32[]{:S(2)}) collective-permute-start(f32[256,512]{1,0:T(8,128)S(1)} %add.174), channel_id=1, source_target_pairs={{8,16},{16,8},{9,17},{17,9},{10,18},{18,10},{11,19},{19,11},{12,20... | collective-permute-start | bytes 1572872 | tf_op jit(solution)/shard_map/ppermute | solution.py:67
  199.3 134.1 %collective-permute-start.7 = (f32[256,512]{1,0:T(8,128)S(1)}, f32[256,512]{1,0:T(8,128)}, u32[]{:S(2)}, u32[]{:S(2)}) collective-permute-start(f32[256,512]{1,0:T(8,128)S(1)} %add.171), channel_id=1, source_target_pairs={{8,0},{16,24},{9,1},{17,25},{10,2},{18,26},{11,3},{19,27},{12,4},{... | collective-permute-start | bytes 1572872 | tf_op jit(solution)/shard_map/ppermute | solution.py:68
  328.2 16.8 %collective-permute-start.10 = (f32[256,512]{1,0:T(8,128)S(1)}, f32[256,512]{1,0:T(8,128)S(1)}, u32[]{:S(2)}, u32[]{:S(2)}) collective-permute-start(f32[256,512]{1,0:T(8,128)S(1)} %add.173), channel_id=1, source_target_pairs={{8,0},{16,24},{9,1},{17,25},{10,2},{18,26},{11,3},{19,27},{12,4},{... | collective-permute-start | bytes 1572872 | tf_op jit(solution)/shard_map/ppermute | solution.py:68
  331.7 22.5 %copy-start = (f32[1024,512]{1,0:T(8,128)S(1)}, f32[1024,512]{1,0:T(8,128)}, u32[]{:S(2)}) copy-start(f32[1024,512]{1,0:T(8,128)} %param.12) | copy-start | bytes 6291460
  331.8 22.5 %copy-start.1 = (f32[1024,512]{1,0:T(8,128)S(1)}, f32[1024,512]{1,0:T(8,128)}, u32[]{:S(2)}) copy-start(f32[1024,512]{1,0:T(8,128)} %param.13) | copy-start | bytes 6291460
  331.8 22.4 %collective-permute-start.13 = (f32[256,512]{1,0:T(8,128)S(1)}, f32[256,512]{1,0:T(8,128)S(1)}, u32[]{:S(2)}, u32[]{:S(2)}) collective-permute-start(f32[256,512]{1,0:T(8,128)S(1)} %add.175), channel_id=1, source_target_pairs={{8,0},{16,24},{9,1},{17,25},{10,2},{18,26},{11,3},{19,27},{12,4},{... | collective-permute-start | bytes 1572872 | tf_op jit(solution)/shard_map/ppermute | solution.py:68
Sparse Core Ops, SparseCore 0:
  31.2 89.0 reduce-scatter.3
  195.0 131.8 all-reduce.3
where the time goes:
time: 365 us; the launch traced here: 364 us
  waiting for transfers between devices  265 us (73%)
  starting transfers between devices  28.8 us (8%)
  other arithmetic  21.1 us (6%)
  between operations  15 us (4%)
  blocking collectives  13.3 us (4%)
  matrix products  10.8 us (3%)
  local copies, waits for them, and re-layouts  10.4 us (3%)
    psum x1, waiting for transfers between devices, body(): totals = lax.psum(padded, everyone)[:partials.shape[0]] / replicas  126 us
    unnamed x3, waiting for transfers between devices  89.2 us
    ppermute x4, waiting for transfers between devices, island_sum(): arrived = lax.ppermute(part, 'island', [(0, 1), (3, 2)])  27.2 us
    ppermute x4, waiting for transfers between devices, island_sum(): back = lax.ppermute(whole, 'island', [(1, 0), (2, 3)])  19.6 us
    ppermute x4, starting transfers between devices, island_sum(): arrived = lax.ppermute(part, 'island', [(0, 1), (3, 2)])  17.6 us
    psum x1, blocking collectives, body(): squares = lax.psum(jnp.sum(gradient * gradient), ('chip', 'core'))  13.3 us
    dot_general x1, matrix products, body(): lax.dot_general(their_unrotated, their_tokens, contract, preferred_elemen...  7.87 us
  transfers between devices with their start and end apart: 16, of which 9 were waited for; matrix products, arithmetic and copies ran while one was open for 4% of the time, Pallas kernels for 0%

commit v1 on v0

--- a/solution.py
+++ b/solution.py
@@ -118,7 +118,7 @@
     everyone = ("island", "chip", "core")
     partials = local_tiles(island_drift, tile_rows, first_row)
     padded = jnp.zeros((65536,), jnp.float32).at[: partials.shape[0]].set(partials)
-    totals = lax.psum(padded, everyone)[: partials.shape[0]] / replicas
+    totals = jnp.sum(lax.all_gather(padded, everyone), axis=0)[: partials.shape[0]] / replicas
     drift = island_sum(island_drift, replicas) / replicas
     momentum_out = outer_moment * momentum + drift
     master_out = master - outer_rate * (drift + outer_moment * momentum_out)

time: 365 us -> 293 us (0.80)
  waiting for transfers between devices: 265 us -> 190 us
  other arithmetic: 21.1 us -> 25.4 us
    psum x1 -> x0, waiting for transfers between devices: 126 us -> none  [body(): totals = lax.psum(padded, everyone)[:partials.shape[0]] / replicas]
    ppermute x4, waiting for transfers between devices: 27.2 us -> 67.4 us  [island_sum(): arrived = lax.ppermute(part, 'island', [(0, 1), (3, 2)])]
    ppermute x4, waiting for transfers between devices: 19.6 us -> 32 us  [island_sum(): back = lax.ppermute(whole, 'island', [(1, 0), (2, 3)])]
    reduce_sum x0 -> x1, other arithmetic: none -> 6.34 us  [body(): jnp.sum(lax.all_gather(padded, everyone), axis=0)[:partials.shape[0]]]
  transfers between devices with their start and end apart: 16 -> 16, of which waited for: 9 -> 9; matrix products, arithmetic and copies ran while one was open for 4% -> 5% of each run, Pallas kernels for 0% -> 0%
where the time goes in v1:
time: 293 us; the launch traced here: 292 us
  waiting for transfers between devices  190 us (65%)
  starting transfers between devices  25.5 us (9%)
  other arithmetic  25.4 us (9%)
  between operations  15.1 us (5%)
  blocking collectives  13.3 us (5%)
  local copies, waits for them, and re-layouts  12.2 us (4%)
  matrix products  10.8 us (4%)
    unnamed x3, waiting for transfers between devices  88.3 us
    ppermute x4, waiting for transfers between devices, island_sum(): arrived = lax.ppermute(part, 'island', [(0, 1), (3, 2)])  67.4 us
    ppermute x4, waiting for transfers between devices, island_sum(): back = lax.ppermute(whole, 'island', [(1, 0), (2, 3)])  32 us
    ppermute x4, starting transfers between devices, island_sum(): arrived = lax.ppermute(part, 'island', [(0, 1), (3, 2)])  16.7 us
    psum x1, blocking collectives, body(): squares = lax.psum(jnp.sum(gradient * gradient), ('chip', 'core'))  13.3 us
    dot_general x1, matrix products, body(): lax.dot_general(their_unrotated, their_tokens, contract, preferred_elemen...  7.87 us
    reduce_sum x1, other arithmetic, local_tiles(): jnp.sum(drift_rows, axis=1)  6.65 us
    reduce_sum x1, other arithmetic, body(): jnp.sum(lax.all_gather(padded, everyone), axis=0)[:partials.shape[0]]  6.34 us
  transfers between devices with their start and end apart: 16, of which 9 were waited for; matrix products, arithmetic and copies ran while one was open for 5% of the time, Pallas kernels for 0%

profile of v1, /device:TPU:0, one launch (start us, length us, event | category | flops | bytes accessed | tf_op | source)
XLA Modules:
  0.0 292.1 jit_solution(3682787724836974566)
XLA Ops:
  7.2 5.7 %dynamic-slice_bitcast_fusion.3 = (bf16[512,1,1024]{2,0,1:T(8,128)(2,1)S(1)}, bf16[512,1,1024]{2,0,1:T(8,128)(2,1)S(1)}, bf16[512,1,1024]{2,0,1:T(8,128)(2,1)S(1...) fusion(bf16[1,512,8192]{2,1,0:T(8,128)(2,1)} %param.10, ...), kind=kLoop, calls=%fused_computation.31 | loop fusion | bytes 16777248 | tf_op jit(solution)/shard_map/stack | solution.py:93
  13.0 2.2 pad_maximum_fusion
  18.4 2.5 fusion
  20.9 2.2 collective-permute-done
  23.1 7.9 %convolution_add_fusion = f32[512,4,1024]{2,0,1:T(8,128)} fusion(f32[512,4,1024]{2,0,1:T(8,128)S(1)} %fusion, bf16[512,4,1024]{2,0,1:T(8,128)(2,1)} %collective-permute-done.1, bf16[512,512]{0,1:T(8,128)(2,1)S(1)} %collective-permute-done), kind=kOutput, calls=%fused_computation.10 | convolution fusion | flops 2149580800 | bytes 21495808 | tf_op jit(solution)/shard_map/dot_general | solution.py:106
  32.0 88.3 %reduce-scatter.4.cloned.1.call-done = f32[512,1,1024]{2,0,1:T(8,128)} async-done(((f32[512,4,1024]{2,0,1:T(8,128)}), f32[512,1,1024]{2,0,1:T(8,128)}) %reduce-scatter.4.cloned.1.call-update) | async-done | bytes 2097168
  120.2 1.9 copy.26
  123.3 13.3 %psum.7 = f32[]{:T(128)} all-reduce(f32[]{:T(128)} %fusion.14), channel_id=1, replica_groups=mesh['island'=4,'chip'=4,'core'=2] {'chip','core'}, use_global_device_ids=true, to_apply=%region_2.3 | all-reduce | flops 1 | bytes 8 | tf_op jit(solution)/shard_map/psum | solution.py:112
  137.3 6.6 %fusion.26 = (f32[1024]{0:T(1024)S(1)}, f32[1024,512]{1,0:T(8,128)}) fusion(f32[1024,512]{1,0:T(8,128)} %param.12, f32[1,1024,512]{2,1,0:T(8,128)} %param.16, f32[]{:T(128)S(6)} %sqrt.9, f32[512,1,1024]{0,2,1:T(8,128)S(1)} %copy.26, f32[1,1024,512]{2,1,0:T(8,128)} %param.15, f32[1,1024,512]{2,1,0:T(8,128)} %param.14), kind=kLoop, calls=%fused_computation.63 | loop fusion | flops 9436160 | bytes 12587012 | tf_op jit(solution)/shard_map/reduce_sum | solution.py:51
  146.2 3.4 %collective-permute-start.2 = (f32[256,512]{1,0:T(8,128)S(1)}, f32[256,512]{1,0:T(8,128)S(1)}, u32[]{:S(2)}, u32[]{:S(2)}) collective-permute-start(f32[256,512]{1,0:T(8,128)S(1)} %slice.41), channel_id=1, source_target_pairs={{0,8},{24,16},{1,9},{25,17},{2,10},{26,18},{3,11},{27,19},{4,12},{... | collective-permute-start | bytes 1572872 | tf_op jit(solution)/shard_map/ppermute | solution.py:65
  149.7 15.2 %collective-permute-done.2 = f32[256,512]{1,0:T(8,128)S(1)} collective-permute-done((f32[256,512]{1,0:T(8,128)S(1)}, f32[256,512]{1,0:T(8,128)S(1)}, u32[]{:S(2)}, u32[]{:S(2)}) %collective-permute-start.2) | collective-permute-done | bytes 524320 | tf_op jit(solution)/shard_map/ppermute | solution.py:65
  164.9 1.8 slice_add_fusion
  166.7 4.4 %collective-permute-start.5 = (f32[256,512]{1,0:T(8,128)S(1)}, f32[256,512]{1,0:T(8,128)S(1)}, u32[]{:S(2)}, u32[]{:S(2)}) collective-permute-start(f32[256,512]{1,0:T(8,128)S(1)} %get-tuple-element.18), channel_id=1, source_target_pairs={{0,8},{24,16},{1,9},{25,17},{2,10},{26,18},{3,11},{27,19},{4,12},{... | collective-permute-start | bytes 1572872 | tf_op jit(solution)/shard_map/ppermute | solution.py:65
  171.1 21.1 %collective-permute-done.5 = f32[256,512]{1,0:T(8,128)S(1)} collective-permute-done((f32[256,512]{1,0:T(8,128)S(1)}, f32[256,512]{1,0:T(8,128)S(1)}, u32[]{:S(2)}, u32[]{:S(2)}) %collective-permute-start.5) | collective-permute-done | bytes 524320 | tf_op jit(solution)/shard_map/ppermute | solution.py:65
  192.3 4.4 %collective-permute-start.8 = (f32[256,512]{1,0:T(8,128)S(1)}, f32[256,512]{1,0:T(8,128)S(1)}, u32[]{:S(2)}, u32[]{:S(2)}) collective-permute-start(f32[256,512]{1,0:T(8,128)S(1)} %get-tuple-element.19), channel_id=1, source_target_pairs={{0,8},{24,16},{1,9},{25,17},{2,10},{26,18},{3,11},{27,19},{4,12},{... | collective-permute-start | bytes 1572872 | tf_op jit(solution)/shard_map/ppermute | solution.py:65
  197.4 15.8 %collective-permute-done.8 = f32[256,512]{1,0:T(8,128)S(1)} collective-permute-done((f32[256,512]{1,0:T(8,128)S(1)}, f32[256,512]{1,0:T(8,128)S(1)}, u32[]{:S(2)}, u32[]{:S(2)}) %collective-permute-start.8) | collective-permute-done | bytes 524320 | tf_op jit(solution)/shard_map/ppermute | solution.py:65
  213.2 4.4 %collective-permute-start.11 = (f32[256,512]{1,0:T(8,128)S(1)}, f32[256,512]{1,0:T(8,128)S(1)}, u32[]{:S(2)}, u32[]{:S(2)}) collective-permute-start(f32[256,512]{1,0:T(8,128)S(1)} %get-tuple-element.20), channel_id=1, source_target_pairs={{0,8},{24,16},{1,9},{25,17},{2,10},{26,18},{3,11},{27,19},{4,12},{... | collective-permute-start | bytes 1572872 | tf_op jit(solution)/shard_map/ppermute | solution.py:65
  220.6 15.3 %collective-permute-done.11 = f32[256,512]{1,0:T(8,128)S(1)} collective-permute-done((f32[256,512]{1,0:T(8,128)S(1)}, f32[256,512]{1,0:T(8,128)S(1)}, u32[]{:S(2)}, u32[]{:S(2)}) %collective-permute-start.11) | collective-permute-done | bytes 524320 | tf_op jit(solution)/shard_map/ppermute | solution.py:65
  240.7 1.6 collective-permute-start.13
  242.3 12.6 %collective-permute-done.7 = f32[256,512]{1,0:T(8,128)} collective-permute-done((f32[256,512]{1,0:T(8,128)S(1)}, f32[256,512]{1,0:T(8,128)}, u32[]{:S(2)}, u32[]{:S(2)}) %collective-permute-start.7) | collective-permute-done | bytes 524320 | tf_op jit(solution)/shard_map/ppermute | solution.py:68
  256.0 9.7 %collective-permute-done.10 = f32[256,512]{1,0:T(8,128)S(1)} collective-permute-done((f32[256,512]{1,0:T(8,128)S(1)}, f32[256,512]{1,0:T(8,128)S(1)}, u32[]{:S(2)}, u32[]{:S(2)}) %collective-permute-start.10) | collective-permute-done | bytes 524320 | tf_op jit(solution)/shard_map/ppermute | solution.py:68
  265.9 9.6 %collective-permute-done.13 = f32[256,512]{1,0:T(8,128)S(1)} collective-permute-done((f32[256,512]{1,0:T(8,128)S(1)}, f32[256,512]{1,0:T(8,128)S(1)}, u32[]{:S(2)}, u32[]{:S(2)}) %collective-permute-start.13) | collective-permute-done | bytes 524320 | tf_op jit(solution)/shard_map/ppermute | solution.py:68
  275.6 2.8 multiply_subtract_fusion
  278.4 6.3 %reduce_sum.29 = f32[65536]{0:T(1024)S(1)} reduce(f32[32,1,65536]{2,1,0:T(1,128)} %all-gather.3.cloned.1.call-done, f32[]{:T(128)} %constant.108.clone.1), dimensions={0,1}, to_apply=%region_5.6 | reduce | flops 2031616 | bytes 8650756 | tf_op jit(solution)/shard_map/reduce_sum | solution.py:121
  (57 shorter events, 17.8 us)
Async XLA Ops:
  7.2 113.1 %reduce-scatter.4.cloned.1.call-start = ((), (), s32[]{:S(2)}) async-start(), calls=%async_computation.2 | async-start | bytes 10485760
  15.2 8.0 %collective-permute-start.1 = (bf16[512,4,1024]{2,0,1:T(8,128)(2,1)}, bf16[512,4,1024]{2,0,1:T(8,128)(2,1)}, u32[]{:S(2)}, u32[]{:S(2)}) collective-permute-start(bf16[512,4,1024]{2,0,1:T(8,128)(2,1)} %pad_maximum_fusion), channel_id=1, source_target_pairs={{0,1},{1,0},{2,3},{3,2},{4,5},{5,4},{6,7},{7,6},{8,9},{9,8},{10,11... | collective-permute-start | bytes 12582920 | tf_op jit(solution)/shard_map/ppermute | solution.py:101
  16.9 1.2 copy-start.2
  16.9 1.5 copy-start.3
  17.7 5.5 %collective-permute-start = (bf16[512,512]{0,1:T(8,128)(2,1)S(1)}, bf16[512,512]{0,1:T(8,128)(2,1)S(1)}, u32[]{:S(2)}, u32[]{:S(2)}) collective-permute-start(bf16[512,512]{0,1:T(8,128)(2,1)S(1)} %bitcast.67), channel_id=1, source_target_pairs={{0,1},{1,0},{2,3},{3,2},{4,5},{5,4},{6,7},{7,6},{8,9},{9,8},{10,11... | collective-permute-start | bytes 1572872 | tf_op jit(solution)/shard_map/ppermute | solution.py:102
  31.0 0.7 copy-start.4
  31.0 247.3 %all-gather.3.cloned.1.call-start = ((), (), s32[]{:S(2)}) async-start(), calls=%async_computation.1 | async-start | bytes 8650752 | tf_op jit(solution)/shard_map/all_gather | solution.py:121
  146.2 18.6 %collective-permute-start.2 = (f32[256,512]{1,0:T(8,128)S(1)}, f32[256,512]{1,0:T(8,128)S(1)}, u32[]{:S(2)}, u32[]{:S(2)}) collective-permute-start(f32[256,512]{1,0:T(8,128)S(1)} %slice.41), channel_id=1, source_target_pairs={{0,8},{24,16},{1,9},{25,17},{2,10},{26,18},{3,11},{27,19},{4,12},{... | collective-permute-start | bytes 1572872 | tf_op jit(solution)/shard_map/ppermute | solution.py:65
  166.7 25.6 %collective-permute-start.5 = (f32[256,512]{1,0:T(8,128)S(1)}, f32[256,512]{1,0:T(8,128)S(1)}, u32[]{:S(2)}, u32[]{:S(2)}) collective-permute-start(f32[256,512]{1,0:T(8,128)S(1)} %get-tuple-element.18), channel_id=1, source_target_pairs={{0,8},{24,16},{1,9},{25,17},{2,10},{26,18},{3,11},{27,19},{4,12},{... | collective-permute-start | bytes 1572872 | tf_op jit(solution)/shard_map/ppermute | solution.py:65
  192.3 20.9 %collective-permute-start.8 = (f32[256,512]{1,0:T(8,128)S(1)}, f32[256,512]{1,0:T(8,128)S(1)}, u32[]{:S(2)}, u32[]{:S(2)}) collective-permute-start(f32[256,512]{1,0:T(8,128)S(1)} %get-tuple-element.19), channel_id=1, source_target_pairs={{0,8},{24,16},{1,9},{25,17},{2,10},{26,18},{3,11},{27,19},{4,12},{... | collective-permute-start | bytes 1572872 | tf_op jit(solution)/shard_map/ppermute | solution.py:65
  196.7 22.5 %collective-permute-start.3 = (f32[256,512]{1,0:T(8,128)S(1)}, f32[256,512]{1,0:T(8,128)S(1)}, u32[]{:S(2)}, u32[]{:S(2)}) collective-permute-start(f32[256,512]{1,0:T(8,128)S(1)} %get-tuple-element.33), channel_id=1, source_target_pairs={{8,16},{16,8},{9,17},{17,9},{10,18},{18,10},{11,19},{19,11},{12,20... | collective-permute-start | bytes 1572872 | tf_op jit(solution)/shard_map/ppermute | solution.py:67
  213.2 22.7 %collective-permute-start.11 = (f32[256,512]{1,0:T(8,128)S(1)}, f32[256,512]{1,0:T(8,128)S(1)}, u32[]{:S(2)}, u32[]{:S(2)}) collective-permute-start(f32[256,512]{1,0:T(8,128)S(1)} %get-tuple-element.20), channel_id=1, source_target_pairs={{0,8},{24,16},{1,9},{25,17},{2,10},{26,18},{3,11},{27,19},{4,12},{... | collective-permute-start | bytes 1572872 | tf_op jit(solution)/shard_map/ppermute | solution.py:65
  217.7 19.0 %collective-permute-start.6 = (f32[256,512]{1,0:T(8,128)S(1)}, f32[256,512]{1,0:T(8,128)S(1)}, u32[]{:S(2)}, u32[]{:S(2)}) collective-permute-start(f32[256,512]{1,0:T(8,128)S(1)} %add.168), channel_id=1, source_target_pairs={{8,16},{16,8},{9,17},{17,9},{10,18},{18,10},{11,19},{19,11},{12,20... | collective-permute-start | bytes 1572872 | tf_op jit(solution)/shard_map/ppermute | solution.py:67
  218.5 19.6 %collective-permute-start.9 = (f32[256,512]{1,0:T(8,128)S(1)}, f32[256,512]{1,0:T(8,128)S(1)}, u32[]{:S(2)}, u32[]{:S(2)}) collective-permute-start(f32[256,512]{1,0:T(8,128)S(1)} %add.170), channel_id=1, source_target_pairs={{8,16},{16,8},{9,17},{17,9},{10,18},{18,10},{11,19},{19,11},{12,20... | collective-permute-start | bytes 1572872 | tf_op jit(solution)/shard_map/ppermute | solution.py:67
  219.3 20.2 %collective-permute-start.4 = (f32[256,512]{1,0:T(8,128)S(1)}, f32[256,512]{1,0:T(8,128)}, u32[]{:S(2)}, u32[]{:S(2)}) collective-permute-start(f32[256,512]{1,0:T(8,128)S(1)} %add.167), channel_id=1, source_target_pairs={{8,0},{16,24},{9,1},{17,25},{10,2},{18,26},{11,3},{19,27},{12,4},{... | collective-permute-start | bytes 1572872 | tf_op jit(solution)/shard_map/ppermute | solution.py:68
  235.9 4.7 %collective-permute-start.12 = (f32[256,512]{1,0:T(8,128)S(1)}, f32[256,512]{1,0:T(8,128)S(1)}, u32[]{:S(2)}, u32[]{:S(2)}) collective-permute-start(f32[256,512]{1,0:T(8,128)S(1)} %add.172), channel_id=1, source_target_pairs={{8,16},{16,8},{9,17},{17,9},{10,18},{18,10},{11,19},{19,11},{12,20... | collective-permute-start | bytes 1572872 | tf_op jit(solution)/shard_map/ppermute | solution.py:67
  236.7 18.2 %collective-permute-start.7 = (f32[256,512]{1,0:T(8,128)S(1)}, f32[256,512]{1,0:T(8,128)}, u32[]{:S(2)}, u32[]{:S(2)}) collective-permute-start(f32[256,512]{1,0:T(8,128)S(1)} %add.169), channel_id=1, source_target_pairs={{8,0},{16,24},{9,1},{17,25},{10,2},{18,26},{11,3},{19,27},{12,4},{... | collective-permute-start | bytes 1572872 | tf_op jit(solution)/shard_map/ppermute | solution.py:68
  238.2 27.6 %collective-permute-start.10 = (f32[256,512]{1,0:T(8,128)S(1)}, f32[256,512]{1,0:T(8,128)S(1)}, u32[]{:S(2)}, u32[]{:S(2)}) collective-permute-start(f32[256,512]{1,0:T(8,128)S(1)} %add.171), channel_id=1, source_target_pairs={{8,0},{16,24},{9,1},{17,25},{10,2},{18,26},{11,3},{19,27},{12,4},{... | collective-permute-start | bytes 1572872 | tf_op jit(solution)/shard_map/ppermute | solution.py:68
  240.7 34.8 %copy-start = (f32[1024,512]{1,0:T(8,128)S(1)}, f32[1024,512]{1,0:T(8,128)}, u32[]{:S(2)}) copy-start(f32[1024,512]{1,0:T(8,128)} %param.12) | copy-start | bytes 6291460
  240.7 34.8 %copy-start.1 = (f32[1024,512]{1,0:T(8,128)S(1)}, f32[1024,512]{1,0:T(8,128)}, u32[]{:S(2)}) copy-start(f32[1024,512]{1,0:T(8,128)} %param.13) | copy-start | bytes 6291460
  240.7 34.7 %collective-permute-start.13 = (f32[256,512]{1,0:T(8,128)S(1)}, f32[256,512]{1,0:T(8,128)S(1)}, u32[]{:S(2)}, u32[]{:S(2)}) collective-permute-start(f32[256,512]{1,0:T(8,128)S(1)} %add.173), channel_id=1, source_target_pairs={{8,0},{16,24},{9,1},{17,25},{10,2},{18,26},{11,3},{19,27},{12,4},{... | collective-permute-start | bytes 1572872 | tf_op jit(solution)/shard_map/ppermute | solution.py:68
Sparse Core Ops, SparseCore 0:
  31.2 89.0 reduce-scatter.3
  145.3 93.9 all-gather.2
